TPU v7x, 256 devices: a whole 4x4x8 slice. The times are simulated.
256 devices in a mesh: dp: 8 (over x_hi, y), seq: 32 (over x_lo, z, core).
Axes of the slice: x: 4 (x_hi: 2, x_lo: 2; x = x_hi * 2 + x_lo), y: 4, z: 8, core: 2. Of those that a mesh axis runs over, the one named last changes fastest.
Arguments:
- tokens: bfloat16 [8, 12288, 2048], P('dp', 'seq'), may hold values from -32 to 32
- w_qkv: bfloat16 [2048, 3072], P(('dp', 'seq')), may hold values from -1 to 1
- w_out: bfloat16 [1024, 2048], P(('dp', 'seq')), may hold values from -0.1875 to 0.1875
Outputs:
- mixed: bfloat16 [8, 12288, 2048], P('dp', 'seq')
All inputs are finite; a program needn't handle non-finite values.
Results may differ from a plain program's by a relative error of at most 0.007.
Values may be sent and summed in bfloat16 or wider, within the bound.
No kernel may reach another device: no remote copies, remote signals or barrier semaphores. Data moves between devices by JAX's collectives and lax.ppermute only.
A program may use at most 64 MiB of HBM per device.

v0:
```python
import math
import jax
import jax.numpy as jnp
from jax import lax
from jax.sharding import PartitionSpec as P

HEADS = 8
HEAD_DIM = 128
COLS = 96


def attend(query, keys, values, allowed):
    scores = jnp.einsum(
        "shqd,shkd->shqk", query, keys, preferred_element_type=jnp.float32
    ) / math.sqrt(query.shape[-1])
    scores = jnp.where(allowed, scores, -jnp.inf)
    top = jnp.max(scores, axis=-1, keepdims=True)
    expo = jnp.exp(scores - top)
    weights = (expo / jnp.sum(expo, axis=-1, keepdims=True)).astype(jnp.bfloat16)
    return jnp.einsum(
        "shqk,shkd->shqd", weights, values, preferred_element_type=jnp.float32
    ).astype(jnp.bfloat16)


def add_rows(left, piece):
    return jnp.dot(left, piece, preferred_element_type=jnp.float32)


def column_heads(packed):
    seq_count, grid_rows, local_cols, count, width = packed.shape
    length = grid_rows * local_cols
    flat = packed.reshape(seq_count, length, count, 3, width // 3)
    flat = jnp.transpose(flat, (0, 2, 3, 1, 4))
    places = jnp.arange(length)
    allowed = (places[:, None] % local_cols == places[None, :] % local_cols) & (
        places[:, None] >= places[None, :]
    )
    result = attend(flat[:, :, 0], flat[:, :, 1], flat[:, :, 2], allowed)
    result = jnp.transpose(result, (0, 2, 1, 3)).reshape(
        seq_count, grid_rows, local_cols, count, width // 3
    )
    return lax.all_to_all(result, "seq", split_axis=1, concat_axis=2, tiled=True)


def on_device(tokens, w_qkv, w_out):
    seq_count, tok_count, width = tokens.shape
    flat = tokens.reshape(seq_count * tok_count, width)
    half = HEADS // 2
    qkv = add_rows(flat, lax.all_gather(w_qkv, ("dp", "seq"), axis=0, tiled=True))
    qkv = qkv.astype(jnp.bfloat16).reshape(seq_count, tok_count, HEADS, 3, HEAD_DIM)
    col_packed = qkv[:, :, half:].reshape(seq_count, tok_count // COLS, COLS, half, 3 * HEAD_DIM)
    col_out = column_heads(
        lax.all_to_all(col_packed, "seq", split_axis=2, concat_axis=1, tiled=True)
    )
    col_out = col_out.reshape(seq_count, tok_count, half, HEAD_DIM)
    row_part = jnp.transpose(qkv[:, :, :half], (0, 2, 3, 1, 4))
    places = jnp.arange(tok_count)
    row_mask = (places[:, None] // COLS == places[None, :] // COLS) & (
        places[:, None] >= places[None, :]
    )
    row_out = attend(row_part[:, :, 0], row_part[:, :, 1], row_part[:, :, 2], row_mask)
    row_out = jnp.transpose(row_out, (0, 2, 1, 3))
    heads_out = jnp.concatenate([row_out, col_out], axis=2).reshape(
        seq_count * tok_count, HEADS * HEAD_DIM
    )
    mixed = add_rows(heads_out, lax.all_gather(w_out, ("dp", "seq"), axis=0, tiled=True))
    return mixed.astype(jnp.bfloat16).reshape(seq_count, tok_count, w_out.shape[1])


def solution(mesh):
    in_specs = (P("dp", "seq", None), P(("dp", "seq"), None), P(("dp", "seq"), None))
    out_specs = P("dp", "seq", None)
    return jax.shard_map(
        on_device, mesh=mesh, in_specs=in_specs, out_specs=out_specs, check_vma=False
    )
```

profile of v0, /device:TPU:32, one launch (start us, length us, event | category | flops | bytes accessed | tf_op | source)
XLA Modules:
  0.0 879.4 jit_solution(4951368546532255029)
XLA Ops:
  6.5 0.0 copy-start
  6.5 0.0 all-gather.4.cloned.1.call-start
  6.5 0.7 all-gather.4.cloned.1.call-update
  7.3 0.0 all-gather.6.cloned.1.call-start
  7.3 0.7 all-gather.6.cloned.1.call-update
  8.0 427.3 %all-gather.4.cloned.1.call-done = bf16[2048,3072]{1,0:T(8,128)(2,1)} async-done(((bf16[8,3072]{1,0:T(8,128)(2,1)}), bf16[2048,3072]{1,0:T(8,128)(2,1)}) %all-gather.4.cloned.1.call-update) | async-done | bytes 12582928 | tf_op jit(solution)/shard_map/all_gather | solution.py:49
  435.3 0.0 copy-done
  435.3 10.9 %convolution_convert_fusion = bf16[384,3072]{1,0:T(8,128)(2,1)} fusion(bf16[2048,3072]{1,0:T(8,128)(2,1)} %all-gather.4.cloned.1.call-done, bf16[1,384,2048]{2,1,0:T(8,128)(2,1)S(1)} %copy-done), kind=kOutput, calls=%fused_computation.2 | convolution fusion | flops 4833017856 | bytes 16515072 | tf_op jit(solution)/shard_map/dot_general | solution.py:26
  446.1 4.3 copy.33
  450.4 3.4 fusion.36
  453.8 3.3 reshape.184
  457.1 2.4 copy.38
  459.5 6.5 all-to-all-start
  466.0 0.1 fusion.14
  466.2 32.2 %all-to-all-done = bf16[1,4,96,4,384]{4,1,3,0,2:T(4,128)(2,1)S(1)} async-done(((bf16[1,4,96,4,384]{4,1,3,0,2:T(4,128)(2,1)}), bf16[1,4,96,4,384]{4,1,3,0,2:T(4,128)(2,1)S(1)}, u32[]{:S(2)}, u32[]{:S(2)}) %all-to-all-start) | async-done | bytes 1179680 | tf_op jit(solution)/shard_map/all_to_all | solution.py:53
  498.4 0.5 copy.39
  498.9 1.4 copy.40
  500.3 3.4 reshape.174
  503.7 1.4 copy.55
  505.1 0.0 copy-start.3
  505.1 2.1 fusion.37
  507.2 0.0 copy-done.3
  507.2 1.3 fusion.7
  508.5 1.1 copy.43
  509.5 4.5 all-to-all-start.1
  514.1 0.1 fusion.15
  514.2 0.0 copy-start.4
  514.2 0.0 copy-start.1
  514.2 339.7 %all-gather.6.cloned.1.call-done = bf16[256,4,2048]{2,1,0:T(4,128)(2,1)} async-done(((bf16[1,4,2048]{2,1,0:T(4,128)(2,1)}), bf16[256,4,2048]{2,1,0:T(4,128)(2,1)}) %all-gather.6.cloned.1.call-update) | async-done | bytes 4194320 | tf_op jit(solution)/shard_map/all_gather | solution.py:66
  854.0 6.9 reshape.183
  860.9 0.0 copy-done.1
  860.9 1.4 copy.53
  862.3 0.0 copy-done.4
  862.3 0.0 copy-start.2
  862.3 2.1 fusion.38
  864.4 0.0 copy-done.2
  864.5 2.1 fusion.6
  866.6 0.0 all-to-all-done.1
  866.6 0.1 copy.45
  866.7 0.3 copy.46
  867.0 0.3 copy.47
  867.3 0.1 pad_maximum_fusion
  867.4 5.2 fusion.2
  (2 shorter events, 0.0 us)
Async XLA Ops:
  6.5 428.7 %copy-start = (bf16[1,384,2048]{2,1,0:T(8,128)(2,1)S(1)}, bf16[1,384,2048]{2,1,0:T(8,128)(2,1)}, u32[]{:S(2)}) copy-start(bf16[1,384,2048]{2,1,0:T(8,128)(2,1)} %param.3) | copy-start | bytes 4718596
  6.5 428.7 %all-gather.4.cloned.1.call-start = ((), (), s32[]{:S(2)}) async-start(), calls=%async_computation.2 | async-start | bytes 12632064 | tf_op jit(solution)/shard_map/all_gather | solution.py:49
  7.3 846.7 %all-gather.6.cloned.1.call-start = ((), (), s32[]{:S(2)}) async-start(), calls=%async_computation.3 | async-start | bytes 4210688 | tf_op jit(solution)/shard_map/all_gather | solution.py:66
  459.5 38.9 %all-to-all-start = ((bf16[1,4,96,4,384]{4,1,3,0,2:T(4,128)(2,1)}), bf16[1,4,96,4,384]{4,1,3,0,2:T(4,128)(2,1)S(1)}, u32[]{:S(2)}, u32[]{:S(2)}) async-start(bf16[1,4,96,4,384]{4,1,3,0,2:T(4,128)(2,1)} %copy.38), calls=%async_computation | async-start | bytes 2359296 | tf_op jit(solution)/shard_map/all_to_all | solution.py:53
  505.1 2.1 copy-start.3
  509.5 357.1 %all-to-all-start.1 = ((bf16[1,128,3,4,128]{4,3,2,0,1:T(4,128)(2,1)}), bf16[1,128,3,4,128]{4,3,2,0,1:T(4,128)(2,1)S(1)}, u32[]{:S(2)}, u32[]{:S(2)}) async-start(bf16[1,128,3,4,128]{4,3,2,0,1:T(4,128)(2,1)} %bitcast.17), calls=%async_computation.1 | async-start | bytes 786432 | tf_op jit(solution)/shard_map/all_to_all | solution.py:42
  514.2 348.1 %copy-start.4 = (pred[384,384]{0,1:T(8,128)(4,1)}, pred[384,384]{0,1:T(8,128)(4,1)S(1)}, u32[]{:S(2)}) copy-start(pred[384,384]{0,1:T(8,128)(4,1)S(1)} %fusion.15) | copy-start | bytes 442372
  514.2 346.6 %copy-start.1 = (bf16[1,384,4,3,128]{1,4,3,2,0:T(8,128)(2,1)S(1)}, bf16[1,384,4,3,128]{1,4,3,2,0:T(8,128)(2,1)}, u32[]{:S(2)}) copy-start(bf16[1,384,4,3,128]{1,4,3,2,0:T(8,128)(2,1)} %get-tuple-element.5) | copy-start | bytes 3538948
  862.3 2.1 copy-start.2
Sparse Core Ops, SparseCore 0:
  9.2 425.9 all-gather.3
  437.1 416.7 all-gather.5
where the time goes:
time: 880 us; the launch traced here: 879 us
  waiting for transfers between devices  801 us (91%)
  local copies, waits for them, and re-layouts  30.1 us (3%)
  matrix products  23.7 us (3%)
  between operations  13.5 us (2%)
  starting transfers between devices  11.1 us (1%)
    all_gather x1, waiting for transfers between devices, on_device(): lax.all_gather(w_qkv, ('dp', 'seq'), axis=0, tiled=True)  427 us
    all_gather x1, waiting for transfers between devices, on_device(): lax.all_gather(w_out, ('dp', 'seq'), axis=0, tiled=True)  340 us
    all_to_all x1, waiting for transfers between devices, on_device(): lax.all_to_all(col_packed, 'seq', split_axis=2, concat_axis=1, tiled=True)  32.2 us
  transfers between devices with their start and end apart: 4, of which 3 were waited for; matrix products, arithmetic and copies ran while one was open for 5% of the time, Pallas kernels for 0%

commit v1 on v0

--- a/solution.py
+++ b/solution.py
@@ -7,6 +7,13 @@
 HEADS = 8
 HEAD_DIM = 128
 COLS = 96
+
+
+def swap_blocks(x, name, split, join):
+    devices = lax.axis_size(name)
+    blocks = jnp.stack(jnp.split(x, devices, axis=split), axis=0)
+    blocks = lax.all_to_all(blocks, name, split_axis=0, concat_axis=0)
+    return jnp.concatenate(blocks, axis=join)
 
 
 def attend(query, keys, values, allowed):
@@ -49,9 +56,7 @@
     qkv = add_rows(flat, lax.all_gather(w_qkv, ("dp", "seq"), axis=0, tiled=True))
     qkv = qkv.astype(jnp.bfloat16).reshape(seq_count, tok_count, HEADS, 3, HEAD_DIM)
     col_packed = qkv[:, :, half:].reshape(seq_count, tok_count // COLS, COLS, half, 3 * HEAD_DIM)
-    col_out = column_heads(
-        lax.all_to_all(col_packed, "seq", split_axis=2, concat_axis=1, tiled=True)
-    )
+    col_out = column_heads(swap_blocks(col_packed, "seq", 2, 1))
     col_out = col_out.reshape(seq_count, tok_count, half, HEAD_DIM)
     row_part = jnp.transpose(qkv[:, :, :half], (0, 2, 3, 1, 4))
     places = jnp.arange(tok_count)

time: 880 us -> 879 us (level)
  waiting for transfers between devices: 801 us -> 693 us
  local copies, waits for them, and re-layouts: 30.1 us -> 135 us
    all_gather x1, waiting for transfers between devices: 340 us -> 234 us  [on_device(): lax.all_gather(w_out, ('dp', 'seq'), axis=0, tiled=True)]
    unnamed x12 -> x107, local copies, waits for them, and re-layouts: 8.37 us -> 94 us
    split x0 -> x2, local copies, waits for them, and re-layouts: none -> 31.5 us  [swap_blocks(): blocks = jnp.stack(jnp.split(x, devices, axis=split), axis=0)]
  transfers between devices with their start and end apart: 4 -> 4, of which waited for: 3 -> 3; matrix products, arithmetic and copies ran while one was open for 5% -> 17% of each run, Pallas kernels for 0% -> 0%
where the time goes in v1:
time: 879 us; the launch traced here: 876 us
  waiting for transfers between devices  693 us (79%)
  local copies, waits for them, and re-layouts  135 us (15%)
  matrix products  20.5 us (2%)
  between operations  13.9 us (2%)
  starting transfers between devices  13 us (1%)
    all_gather x1, waiting for transfers between devices, on_device(): lax.all_gather(w_qkv, ('dp', 'seq'), axis=0, tiled=True)  427 us
    all_gather x1, waiting for transfers between devices, on_device(): lax.all_gather(w_out, ('dp', 'seq'), axis=0, tiled=True)  234 us
    unnamed x107, local copies, waits for them, and re-layouts  94 us
    split x2, local copies, waits for them, and re-layouts, swap_blocks(): blocks = jnp.stack(jnp.split(x, devices, axis=split), axis=0)  31.5 us
    all_to_all x1, waiting for transfers between devices, swap_blocks(): blocks = lax.all_to_all(blocks, name, split_axis=0, concat_axis=0)  30.4 us
  transfers between devices with their start and end apart: 4, of which 3 were waited for; matrix products, arithmetic and copies ran while one was open for 17% of the time, Pallas kernels for 0%

profile of v1, /device:TPU:32, one launch (start us, length us, event | category | flops | bytes accessed | tf_op | source)
XLA Modules:
  0.0 876.1 jit_solution(8757345693403767040)
XLA Ops:
  8.0 427.3 %all-gather.4.cloned.1.call-done = bf16[2048,3072]{1,0:T(8,128)(2,1)} async-done(((bf16[8,3072]{1,0:T(8,128)(2,1)}), bf16[2048,3072]{1,0:T(8,128)(2,1)}) %all-gather.4.cloned.1.call-update) | async-done | bytes 12582928 | tf_op jit(solution)/shard_map/all_gather | solution.py:56
  435.3 10.8 %convolution_convert_fusion = bf16[384,3072]{1,0:T(8,128)(2,1)} fusion(bf16[2048,3072]{1,0:T(8,128)(2,1)} %all-gather.4.cloned.1.call-done, bf16[1,384,2048]{2,1,0:T(8,128)(2,1)S(1)} %copy-done), kind=kOutput, calls=%fused_computation.2 | convolution fusion | flops 4833017856 | bytes 16515072 | tf_op jit(solution)/shard_map/dot_general | solution.py:33
  446.1 3.0 copy.20
  449.1 1.3 fusion.36
  450.4 1.2 reshape.179
  451.6 12.6 %fusion.38 = (bf16[1,4,3,4,384]{2,1,4,3,0:T(4,128)(2,1)S(1)}, bf16[1,4,3,4,384]{2,1,4,3,0:T(4,128)(2,1)}, bf16[1,4,3,4,384]{2,1,4,3,0:T(4,128)(2,1)}, bf16[1,4,3...) fusion(bf16[1,4,96,4,384]{2,1,4,3,0:T(4,128)(2,1)S(1)} %reshape.179), kind=kLoop, calls=%fused_computation.91 | loop fusion | bytes 958464 | tf_op jit(solution)/shard_map/split | solution.py:14
  464.3 18.9 %fusion.37 = (bf16[1,4,3,4,384]{2,1,4,3,0:T(4,128)(2,1)}, bf16[1,4,3,4,384]{2,1,4,3,0:T(4,128)(2,1)}, bf16[1,4,3,4,384]{2,1,4,3,0:T(4,128)(2,1)}, bf16[1,4,3,4,3...) fusion(bf16[1,4,96,4,384]{2,1,4,3,0:T(4,128)(2,1)S(1)} %reshape.179), kind=kLoop, calls=%fused_computation.90 | loop fusion | bytes 1400832 | tf_op jit(solution)/shard_map/split | solution.py:14
  483.2 2.9 copy.38
  486.8 2.8 copy.39
  489.6 0.8 copy.40
  490.5 2.9 copy.41
  493.4 2.8 copy.42
  496.2 0.8 copy.43
  497.1 2.9 copy.44
  500.0 2.8 copy.45
  502.9 0.8 copy.46
  508.8 3.5 copy.47
  512.3 3.4 copy.48
  515.7 1.7 copy.49
  517.5 1.8 copy.50
  519.2 1.7 copy.51
  521.0 3.5 copy.52
  524.5 1.7 copy.53
  526.3 1.7 copy.54
  528.0 3.5 copy.55
  531.5 1.7 copy.56
  533.3 1.7 copy.57
  535.0 3.5 copy.58
  538.6 1.7 copy.59
  540.3 1.7 copy.60
  542.0 3.5 copy.61
  546.4 0.8 copy.63
  547.3 2.9 copy.64
  550.2 0.8 copy.65
  552.0 2.9 copy.67
  554.9 0.8 copy.68
  569.9 1.5 copy.25
  571.4 6.6 all-to-all-start
  578.1 30.4 %all-to-all-done = bf16[32,1,4,3,4,384]{5,4,3,2,1,0:T(4,128)(2,1)S(1)} async-done(((bf16[32,1,4,3,4,384]{5,4,3,2,1,0:T(4,128)(2,1)}), bf16[32,1,4,3,4,384]{5,4,3,2,1,0:T(4,128)(2,1)S(1)}, u32[]{:S(2)}, u32[]{:S(2)}) %all-to-all-start) | async-done | bytes 1179680 | tf_op jit(solution)/shard_map/all_to_all | solution.py:15
  609.4 0.9 fusion.39
  610.3 1.3 fusion.7
  611.6 1.1 copy.28
  612.7 6.4 all-to-all-start.1
  619.2 234.1 %all-gather.6.cloned.1.call-done = bf16[256,4,2048]{2,1,0:T(4,128)(2,1)} async-done(((bf16[1,4,2048]{2,1,0:T(4,128)(2,1)}), bf16[256,4,2048]{2,1,0:T(4,128)(2,1)}) %all-gather.6.cloned.1.call-update) | async-done | bytes 4194320 | tf_op jit(solution)/shard_map/all_gather | solution.py:71
  853.3 6.9 reshape.178
  861.0 0.9 fusion.40
  861.9 1.2 fusion.6
  863.9 5.3 fusion.2
  (93 shorter events, 25.6 us)
Async XLA Ops:
  6.5 428.7 %copy-start = (bf16[1,384,2048]{2,1,0:T(8,128)(2,1)S(1)}, bf16[1,384,2048]{2,1,0:T(8,128)(2,1)}, u32[]{:S(2)}) copy-start(bf16[1,384,2048]{2,1,0:T(8,128)(2,1)} %param.3) | copy-start | bytes 4718596
  6.5 428.7 %all-gather.4.cloned.1.call-start = ((), (), s32[]{:S(2)}) async-start(), calls=%async_computation.2 | async-start | bytes 12632064 | tf_op jit(solution)/shard_map/all_gather | solution.py:56
  7.3 846.0 %all-gather.6.cloned.1.call-start = ((), (), s32[]{:S(2)}) async-start(), calls=%async_computation.3 | async-start | bytes 4210688 | tf_op jit(solution)/shard_map/all_gather | solution.py:71
  483.2 6.4 copy-start.5
  490.5 5.8 copy-start.4
  497.1 5.8 copy-start.3
  508.8 6.9 copy-start.2
  517.5 1.8 copy-start.18
  519.2 5.3 copy-start.17
  521.0 5.3 copy-start.16
  526.3 5.3 copy-start.15
  528.0 5.3 copy-start.14
  533.3 5.3 copy-start.13
  535.0 5.3 copy-start.12
  540.3 5.3 copy-start.11
  542.0 4.4 copy-start.10
  546.4 3.8 copy-start.9
  547.3 3.8 copy-start.8
  551.1 3.8 copy-start.7
  552.0 3.8 copy-start.6
  555.8 1.4 copy-start.20
  571.4 37.1 %all-to-all-start = ((bf16[32,1,4,3,4,384]{5,4,3,2,1,0:T(4,128)(2,1)}), bf16[32,1,4,3,4,384]{5,4,3,2,1,0:T(4,128)(2,1)S(1)}, u32[]{:S(2)}, u32[]{:S(2)}) async-start(bf16[32,1,4,3,4,384]{5,4,3,2,1,0:T(4,128)(2,1)} %copy.25), calls=%async_computation | async-start | bytes 2359296 | tf_op jit(solution)/shard_map/all_to_all | solution.py:15
  612.7 250.5 %all-to-all-start.1 = ((bf16[1,128,3,4,128]{4,3,2,0,1:T(4,128)(2,1)}), bf16[1,128,3,4,128]{4,3,2,0,1:T(4,128)(2,1)S(1)}, u32[]{:S(2)}, u32[]{:S(2)}) async-start(bf16[1,128,3,4,128]{4,3,2,0,1:T(4,128)(2,1)} %bitcast.47), calls=%async_computation.1 | async-start | bytes 786432 | tf_op jit(solution)/shard_map/all_to_all | solution.py:49
  619.2 241.0 %copy-start.19 = (bf16[1,384,4,3,128]{1,4,3,2,0:T(8,128)(2,1)S(1)}, bf16[1,384,4,3,128]{1,4,3,2,0:T(8,128)(2,1)}, u32[]{:S(2)}) copy-start(bf16[1,384,4,3,128]{1,4,3,2,0:T(8,128)(2,1)} %get-tuple-element.5) | copy-start | bytes 3538948
  863.9 5.3 copy-start.1
Sparse Core Ops, SparseCore 0:
  9.2 425.9 all-gather.3
  437.1 416.1 all-gather.5
